TPU v7x, 32 devices: a whole 2x2x4 slice. The times are simulated.
32 devices in a mesh: dp: 4 (over y, x), seq: 8 (over z, core).
Axes of the slice: x: 2, y: 2, z: 4, core: 2. Of those that a mesh axis runs over, the one named last changes fastest.
Arguments:
- queries: bfloat16 [4, 8, 512, 2048], P('dp', 'seq'), may hold values from -48 to 48
- keys: bfloat16 [4, 8, 512, 2048], P('dp', 'seq'), may hold values from -6 to 6
- values: bfloat16 [4, 8, 512, 2048], P('dp', 'seq'), may hold values from -6 to 6
- out_grad: bfloat16 [4, 8, 512, 2048], P('dp', 'seq'), may hold values from -6 to 6
- out_weight: bfloat16 [2048, 2048], P('dp'), may hold values from -0.125 to 0.125
- row_mask: int32 [4, 4], replicated, may hold values from 0 to 1, as said below
- col_mask: int32 [8, 8], replicated, may hold values from 0 to 1, as said below
Outputs:
- layer_out: bfloat16 [4, 8, 512, 2048], P('dp', 'seq')
- query_grad: bfloat16 [4, 8, 512, 2048], P('dp', 'seq')
- key_grad: bfloat16 [4, 8, 512, 2048], P('dp', 'seq')
- value_grad: bfloat16 [4, 8, 512, 2048], P('dp', 'seq')
- wo_grad: float32 [2048, 2048], P(('dp', 'seq'))
Inputs may be any that keep to these rules, and one draw needn't show every extreme that they name: row_mask[a, b] is 1 for b = a and 0 for b > a. col_mask[r, s] is 1 for s = r and for s = r - 1, and 0 for s > r.
All inputs are finite; a program needn't handle non-finite values.
Results may differ from a plain program's by a relative error of at most 0.012.
Values may be sent and summed in bfloat16 or wider, within the bound.
No kernel may reach another device: no remote copies, remote signals or barrier semaphores. Data moves between devices by JAX's collectives and lax.ppermute only.
A program may use at most 192 MiB of HBM per device.

v0:
```python
import math
import jax
import jax.numpy as jnp
from jax import lax
from jax.sharding import PartitionSpec as P

DH = 128
COLS = 512
BLK = 128
masked_out = -1e30
scale = 1.0 / math.sqrt(DH)


def row_permit(row_mask):
    spread = jnp.repeat(jnp.repeat(row_mask, BLK, axis=0), BLK, axis=1)
    row_index = lax.broadcasted_iota(jnp.int32, (COLS, COLS), 0)
    col_index = lax.broadcasted_iota(jnp.int32, (COLS, COLS), 1)
    return (spread == 1) & (col_index <= row_index)


def softmax_parts(scores, allowed):
    highest = jnp.max(jnp.where(allowed, scores, masked_out), axis=-1, keepdims=True)
    attend = jnp.exp(jnp.where(allowed, scores - highest, masked_out))
    totals = jnp.sum(attend, axis=-1, keepdims=True)
    probs = (attend / totals).astype(jnp.bfloat16)
    return (probs, highest + jnp.log(totals))


def row_forward(q, k, v, allowed):
    scores = jnp.einsum("ihd,jhd->hij", q, k, preferred_element_type=jnp.float32) * scale
    probs, log_total = softmax_parts(scores, allowed[None])
    out = jnp.einsum("hij,jhd->ihd", probs, v, preferred_element_type=jnp.float32)
    return (out.astype(jnp.bfloat16), scores, log_total)


def row_backward(q, k, v, out, grad, scores, log_total, allowed):
    grad_dot = jnp.einsum("ihd,ihd->hi", grad, out, preferred_element_type=jnp.float32)
    back = jnp.where(allowed[None], jnp.exp(scores - log_total), 0.0)
    value_grad = jnp.einsum(
        "hij,ihd->jhd", back.astype(jnp.bfloat16), grad, preferred_element_type=jnp.float32
    )
    prob_grad = jnp.einsum("ihd,jhd->hij", grad, v, preferred_element_type=jnp.float32)
    score_grad = (back * (prob_grad - grad_dot[..., None])).astype(jnp.bfloat16)
    query_grad = jnp.einsum("hij,jhd->ihd", score_grad, k, preferred_element_type=jnp.float32)
    key_grad = jnp.einsum("hij,ihd->jhd", score_grad, q, preferred_element_type=jnp.float32)
    return tuple(
        (g.astype(jnp.bfloat16) for g in (query_grad * scale, key_grad * scale, value_grad))
    )


def column_forward(q, k, v, allowed):
    scores = jnp.einsum("rchd,schd->chrs", q, k, preferred_element_type=jnp.float32) * scale
    probs, log_total = softmax_parts(scores, allowed)
    out = jnp.einsum("chrs,schd->rchd", probs, v, preferred_element_type=jnp.float32)
    return (out.astype(jnp.bfloat16), scores, log_total)


def column_backward(q, k, v, out, grad, scores, log_total, allowed):
    grad_dot = jnp.einsum("rchd,rchd->chr", grad, out, preferred_element_type=jnp.float32)
    back = jnp.where(allowed, jnp.exp(scores - log_total), 0.0)
    value_grad = jnp.einsum(
        "chrs,rchd->schd", back.astype(jnp.bfloat16), grad, preferred_element_type=jnp.float32
    )
    prob_grad = jnp.einsum("rchd,schd->chrs", grad, v, preferred_element_type=jnp.float32)
    score_grad = (back * (prob_grad - grad_dot[..., None])).astype(jnp.bfloat16)
    query_grad = jnp.einsum("chrs,schd->rchd", score_grad, k, preferred_element_type=jnp.float32)
    key_grad = jnp.einsum("chrs,rchd->schd", score_grad, q, preferred_element_type=jnp.float32)
    return tuple(
        (g.astype(jnp.bfloat16) for g in (query_grad * scale, key_grad * scale, value_grad))
    )


def on_device(queries, keys, values, out_grad, out_weight, row_mask, col_mask):
    tokens, features = (queries.shape[2], queries.shape[3])
    half = features // 2
    heads_half = half // DH
    rows = lax.axis_size("seq")
    cols_each = tokens // rows
    weight = lax.all_gather(out_weight, "dp", axis=0, tiled=True)
    chunks = 2
    piece = cols_each // chunks

    def chunked(t):
        return t.reshape(rows, chunks, piece, half).transpose(1, 0, 2, 3)

    packed = jnp.stack([chunked(t[0, 0, :, half:]) for t in (queries, keys, values)], axis=1)
    col_ok = col_mask == 1
    shipped_all = [
        lax.all_to_all(packed[j], "seq", split_axis=1, concat_axis=1, tiled=True)
        for j in range(chunks)
    ]
    row_ok = row_permit(row_mask)
    split = lambda t: t[0, 0, :, :half].reshape(tokens, heads_half, DH)
    row_q, row_k, row_v = (split(queries), split(keys), split(values))
    row_out, row_scores, row_total = row_forward(row_q, row_k, row_v, row_ok)
    row_attn = row_out.reshape(tokens, half)
    flat_grad = out_grad[0, 0]
    contract = (((0,), (0,)), ((), ()))
    row_done, shipped_first = lax.optimization_barrier(
        ((row_out, row_scores, row_total), shipped_all[0])
    )
    row_out, row_scores, row_total = row_done
    row_attn = row_out.reshape(tokens, half)
    shipped_all[0] = shipped_first
    col_state = []
    col_back = []
    for j in range(chunks):
        shipped = shipped_all[j]
        col_q, col_k, col_v = (shipped[i].reshape(rows, piece, heads_half, DH) for i in range(3))
        col_out, col_scores, col_total = column_forward(col_q, col_k, col_v, col_ok)
        col_state.append((col_q, col_k, col_v, col_out, col_scores, col_total))
        col_back.append(col_out.reshape(rows, piece, half))
    col_attn = lax.all_to_all(
        jnp.stack(col_back, axis=1), "seq", split_axis=0, concat_axis=0, tiled=True
    ).reshape(tokens, half)
    attention = jnp.concatenate([row_attn, col_attn], axis=1)
    partial = lax.dot_general(attention, flat_grad, contract, preferred_element_type=jnp.float32)
    by_rows_of = (((1,), (1,)), ((), ()))
    row_grad = lax.dot_general(
        flat_grad, weight[:half], by_rows_of, preferred_element_type=jnp.float32
    ).astype(jnp.bfloat16)
    partial, late_weight = lax.optimization_barrier((partial, weight))
    col_grad = lax.dot_general(
        flat_grad, late_weight[half:], by_rows_of, preferred_element_type=jnp.float32
    ).astype(jnp.bfloat16)
    grad_col_part = chunked(col_grad)
    devices_all = lax.axis_size(("dp", "seq"))
    wo_grad = lax.psum_scatter(
        partial.astype(jnp.bfloat16), ("dp", "seq"), scatter_dimension=0, tiled=True
    ).astype(jnp.float32) * (1.0 / math.sqrt(tokens * devices_all))
    col_grads_back = []
    for j in range(chunks):
        grad_cols = lax.all_to_all(
            grad_col_part[j], "seq", split_axis=0, concat_axis=0, tiled=True
        ).reshape(rows, piece, heads_half, DH)
        col_q, col_k, col_v, col_out, col_scores, col_total = col_state[j]
        col_grads = column_backward(
            col_q, col_k, col_v, col_out, grad_cols, col_scores, col_total, col_ok
        )
        col_grads_back.append(
            lax.all_to_all(
                jnp.stack([g.reshape(rows, piece, half) for g in col_grads]),
                "seq",
                split_axis=1,
                concat_axis=1,
                tiled=True,
            )
        )
    col_grads_whole = jnp.stack(col_grads_back, axis=2).reshape(3, tokens, half)
    row_grads = row_backward(
        row_q,
        row_k,
        row_v,
        row_out,
        row_grad.reshape(tokens, heads_half, DH),
        row_scores,
        row_total,
        row_ok,
    )
    layer_out = jnp.dot(attention, weight, preferred_element_type=jnp.float32).astype(jnp.bfloat16)
    grads = [
        jnp.concatenate([row_grads[i].reshape(tokens, half), col_grads_whole[i]], axis=1)[
            None, None
        ]
        for i in range(3)
    ]
    return (layer_out[None, None], grads[0], grads[1], grads[2], wo_grad)


def solution(mesh):
    in_specs = (
        P("dp", "seq", None, None),
        P("dp", "seq", None, None),
        P("dp", "seq", None, None),
        P("dp", "seq", None, None),
        P("dp", None),
        P(),
        P(),
    )
    out_specs = (
        P("dp", "seq", None, None),
        P("dp", "seq", None, None),
        P("dp", "seq", None, None),
        P("dp", "seq", None, None),
        P(("dp", "seq"), None),
    )
    return jax.shard_map(
        on_device, mesh=mesh, in_specs=in_specs, out_specs=out_specs, check_vma=False
    )
```

profile of v0, /device:TPU:0, one launch (start us, length us, event | category | flops | bytes accessed | tf_op | source)
XLA Modules:
  0.0 367.7 jit_solution(15175648478473161992)
XLA Ops:
  7.9 1.9 fusion.99
  12.8 1.6 slice_bitcast_fusion.1
  15.7 6.3 %all-to-all-start.1 = ((bf16[3,8,32,1024]{3,2,0,1:T(8,128)(2,1)}), bf16[3,8,32,1024]{3,2,0,1:T(8,128)(2,1)}, u32[]{:S(2)}, u32[]{:S(2)}) async-start(bf16[3,8,32,1024]{3,2,0,1:T(8,128)(2,1)} %copy.219), calls=%async_computation.1 | async-start | bytes 3145728 | tf_op jit(solution)/shard_map/all_to_all | solution.py:89
  22.4 1.3 copy.295
  23.7 1.6 copy.296
  25.3 2.7 copy.297
  28.0 2.7 copy.211
  30.7 29.2 %all-to-all-done.1 = bf16[3,8,32,1024]{3,2,0,1:T(8,128)(2,1)} async-done(((bf16[3,8,32,1024]{3,2,0,1:T(8,128)(2,1)}), bf16[3,8,32,1024]{3,2,0,1:T(8,128)(2,1)}, u32[]{:S(2)}, u32[]{:S(2)}) %all-to-all-start.1) | async-done | bytes 1572896 | tf_op jit(solution)/shard_map/all_to_all | solution.py:89
  59.9 4.6 %all-to-all-start = ((bf16[3,8,32,1024]{3,2,0,1:T(8,128)(2,1)}), bf16[3,8,32,1024]{3,2,0,1:T(8,128)(2,1)}, u32[]{:S(2)}, u32[]{:S(2)}) async-start(bf16[3,8,32,1024]{3,2,0,1:T(8,128)(2,1)} %copy.211), calls=%async_computation | async-start | bytes 3145728 | tf_op jit(solution)/shard_map/all_to_all | solution.py:89
  64.5 2.9 select_reduce_fusion
  67.4 1.5 fusion
  70.7 3.6 fusion.36
  74.3 1.5 fusion.102
  78.5 23.8 %all-to-all-done = bf16[3,8,32,1024]{3,2,0,1:T(8,128)(2,1)} async-done(((bf16[3,8,32,1024]{3,2,0,1:T(8,128)(2,1)}), bf16[3,8,32,1024]{3,2,0,1:T(8,128)(2,1)}, u32[]{:S(2)}, u32[]{:S(2)}) %all-to-all-start) | async-done | bytes 1572896 | tf_op jit(solution)/shard_map/all_to_all | solution.py:89
  102.3 1.5 fusion.101
  106.0 2.0 fusion.54
  110.9 2.1 stack_reshape.25
  113.0 2.1 convolution_convert_fusion.4
  116.7 2.0 stack_reshape.24
  121.2 4.2 %all-to-all-start.2 = ((bf16[8,2,32,1024]{3,2,1,0:T(8,128)(2,1)}), bf16[8,2,32,1024]{3,2,1,0:T(8,128)(2,1)}, u32[]{:S(2)}, u32[]{:S(2)}) async-start(bf16[8,2,32,1024]{3,2,1,0:T(8,128)(2,1)} %copy.225), calls=%async_computation.2 | async-start | bytes 2097152 | tf_op jit(solution)/shard_map/all_to_all | solution.py:113
  126.0 2.3 copy.212
  128.3 23.7 %all-to-all-done.2 = bf16[8,2,32,1024]{3,2,1,0:T(8,128)(2,1)} async-done(((bf16[8,2,32,1024]{3,2,1,0:T(8,128)(2,1)}), bf16[8,2,32,1024]{3,2,1,0:T(8,128)(2,1)}, u32[]{:S(2)}, u32[]{:S(2)}) %all-to-all-start.2) | async-done | bytes 1048608 | tf_op jit(solution)/shard_map/all_to_all | solution.py:113
  152.0 2.3 copy.226
  154.3 8.3 %fusion.14 = bf16[2048,2048]{1,0:T(8,128)(2,1)} fusion(bf16[1,1,512,2048]{3,2,1,0:T(8,128)(2,1)S(1)} %copy-done, bf16[512,1024]{0,1:T(8,128)(2,1)} %copy.226, bf16[512,1024]{0,1:T(8,128)(2,1)} %bitcast.241), kind=kOutput, calls=%fused_computation.29 | convolution fusion | flops 4299161600 | bytes 12582912 | tf_op jit(solution)/shard_map/dot_general | solution.py:117
  162.6 4.5 %fusion.18 = bf16[1024,512]{0,1:T(8,128)(2,1)S(1)} fusion(bf16[1,1,512,2048]{3,2,1,0:T(8,128)(2,1)S(1)} %copy-done, bf16[2048,2048]{1,0:T(8,128)(2,1)} %all-gather.2.cloned.1.call-done), kind=kOutput, calls=%fused_computation.42 | convolution fusion | flops 2148007936 | bytes 7340032 | tf_op jit(solution)/shard_map/dot_general | solution.py:123
  168.4 4.2 %all-to-all-start.3 = ((bf16[8,32,1024]{2,1,0:T(8,128)(2,1)}), bf16[8,32,1024]{2,1,0:T(8,128)(2,1)}, u32[]{:S(2)}, u32[]{:S(2)}) async-start(bf16[8,32,1024]{2,1,0:T(8,128)(2,1)} %get-tuple-element.37), calls=%async_computation.3 | async-start | bytes 1048576 | tf_op jit(solution)/shard_map/all_to_all | solution.py:133
  172.5 1.8 log_add_fusion
  174.3 20.8 %all-to-all-done.3 = bf16[8,32,1024]{2,1,0:T(8,128)(2,1)} async-done(((bf16[8,32,1024]{2,1,0:T(8,128)(2,1)}), bf16[8,32,1024]{2,1,0:T(8,128)(2,1)}, u32[]{:S(2)}, u32[]{:S(2)}) %all-to-all-start.3) | async-done | bytes 524320 | tf_op jit(solution)/shard_map/all_to_all | solution.py:133
  195.1 4.2 %all-to-all-start.5 = ((bf16[8,32,1024]{2,1,0:T(8,128)(2,1)}), bf16[8,32,1024]{2,1,0:T(8,128)(2,1)}, u32[]{:S(2)}, u32[]{:S(2)}) async-start(bf16[8,32,1024]{2,1,0:T(8,128)(2,1)} %get-tuple-element.36), calls=%async_computation.5 | async-start | bytes 1048576 | tf_op jit(solution)/shard_map/all_to_all | solution.py:133
  201.2 1.9 fusion.49
  203.9 2.1 stack_reshape.28
  207.3 1.7 multiply_reduce_fusion.2
  212.1 2.1 stack_reshape.26
  214.2 1.7 fusion.47
  216.8 2.1 stack_reshape.27
  218.9 1.5 pad_maximum_fusion.2
  220.4 1.3 copy.242
  223.0 4.5 %all-to-all-start.4 = ((bf16[3,8,32,1024]{3,2,0,1:T(8,128)(2,1)}), bf16[3,8,32,1024]{3,2,0,1:T(8,128)(2,1)}, u32[]{:S(2)}, u32[]{:S(2)}) async-start(bf16[3,8,32,1024]{3,2,0,1:T(8,128)(2,1)} %copy.242), calls=%async_computation.4 | async-start | bytes 3145728 | tf_op jit(solution)/shard_map/all_to_all | solution.py:141
  227.5 4.6 %fusion.31 = bf16[64,8,8,128]{3,1,2,0:T(8,128)(2,1)S(1)} fusion(bf16[2048,2048]{1,0:T(8,128)(2,1)} %all-gather.2.cloned.1.call-done, bf16[1,1,512,2048]{3,2,1,0:T(8,128)(2,1)S(1)} %copy-done), kind=kOutput, calls=%fused_computation.45 | convolution fusion | flops 2148007936 | bytes 7340032 | tf_op jit(solution)/shard_map/dot_general | solution.py:119
  233.4 2.4 copy.259
  235.8 1.4 bitcast_convert_fusion
  241.6 2.1 stack_reshape.31
  244.9 1.7 multiply_reduce_fusion.1
  249.8 2.1 stack_reshape.29
  251.9 1.6 fusion.45
  253.7 1.4 pad_maximum_fusion.3
  255.1 1.3 copy.254
  256.5 26.0 %all-to-all-done.4 = bf16[3,8,32,1024]{3,2,0,1:T(8,128)(2,1)} async-done(((bf16[3,8,32,1024]{3,2,0,1:T(8,128)(2,1)}), bf16[3,8,32,1024]{3,2,0,1:T(8,128)(2,1)}, u32[]{:S(2)}, u32[]{:S(2)}) %all-to-all-start.4) | async-done | bytes 1572896 | tf_op jit(solution)/shard_map/all_to_all | solution.py:141
  282.4 5.8 %all-to-all-start.6 = ((bf16[3,8,32,1024]{3,2,0,1:T(8,128)(2,1)}), bf16[3,8,32,1024]{3,2,0,1:T(8,128)(2,1)}, u32[]{:S(2)}, u32[]{:S(2)}) async-start(bf16[3,8,32,1024]{3,2,0,1:T(8,128)(2,1)} %copy.254), calls=%async_computation.6 | async-start | bytes 3145728 | tf_op jit(solution)/shard_map/all_to_all | solution.py:141
  288.3 5.5 %multiply_convert_fusion = bf16[8,512,512]{1,2,0:T(8,128)(2,1)S(1)} fusion(f32[8,512,512]{1,2,0:T(8,128)} %copy-done.1, f32[8,512]{1,0:T(8,128)S(1)} %multiply_reduce_fusion, f32[8,512]{1,0:T(8,128)S(1)} %bitcast.246, pred[512,512]{0,1:T(8,128)(4,1)S(1)} %fusion.53, bf16[512,8,128]{0,2,1:T(8,128)(2,1)} %copy.259, bf16[512,8,128]{0,2,1:T(8,128)(2,1)S(1)} %bitcast.214), kind=kOutput, calls=%fused_computation | convolution fusion | flops 547356672 | bytes 14974976 | tf_op jit(solution)/shard_map/ihd,jhd->hij/dot_general | solution.py:42
  295.9 1.3 copy.256
  297.2 5.1 %multiply_convert_fusion.1 = bf16[8,512,128]{1,2,0:T(8,128)(2,1)} fusion(bf16[8,512,512]{1,2,0:T(8,128)(2,1)} %copy-done.2, bf16[512,8,128]{0,2,1:T(8,128)(2,1)} %bitcast.224), kind=kOutput, calls=%fused_computation.33 | convolution fusion | flops 537919488 | bytes 6291456 | tf_op jit(solution)/shard_map/hij,ihd->jhd/dot_general | solution.py:45
  302.3 2.3 copy.258
  304.6 6.0 %fusion.28 = bf16[8,128,512]{2,1,0:T(8,128)(2,1)} fusion(bf16[512,8,128]{0,2,1:T(8,128)(2,1)S(1)} %copy-done.20, f32[8,512,512]{1,2,0:T(8,128)} %copy-done.1, f32[8,512]{1,0:T(8,128)S(1)} %bitcast.247, pred[512,512]{0,1:T(8,128)(4,1)S(1)} %fusion.53), kind=kOutput, calls=%fused_computation.44 | convolution fusion | flops 543686656 | bytes 10764288 | tf_op jit(solution)/shard_map/hij,ihd->jhd/dot_general | solution.py:39
  310.6 1.5 copy.261
  312.1 10.0 %fusion.12 = bf16[1,1,512,2048]{3,2,1,0:T(8,128)(2,1)} fusion(bf16[2048,2048]{1,0:T(8,128)(2,1)} %all-gather.2.cloned.1.call-done, bf16[512,1024]{0,1:T(8,128)(2,1)} %copy.226, bf16[512,1024]{0,1:T(8,128)(2,1)} %bitcast.242), kind=kOutput, calls=%fused_computation.23 | convolution fusion | flops 4300210176 | bytes 12582912 | tf_op jit(solution)/shard_map/dot_general | solution.py:160
  322.0 2.8 copy.356
  324.8 19.7 %all-to-all-done.6 = bf16[3,8,32,1024]{3,2,0,1:T(8,128)(2,1)} async-done(((bf16[3,8,32,1024]{3,2,0,1:T(8,128)(2,1)}), bf16[3,8,32,1024]{3,2,0,1:T(8,128)(2,1)}, u32[]{:S(2)}, u32[]{:S(2)}) %all-to-all-start.6) | async-done | bytes 1572896 | tf_op jit(solution)/shard_map/all_to_all | solution.py:141
  344.5 1.7 copy.355
  346.7 1.5 maximum_bitcast_fusion.2
  348.2 1.5 maximum_bitcast_fusion
  349.7 1.5 maximum_bitcast_fusion.1
  351.2 7.6 %reduce-scatter.2.cloned.1.call-done = bf16[64,2048]{1,0:T(8,128)(2,1)} async-done(((bf16[2048,2048]{1,0:T(8,128)(2,1)}), bf16[64,2048]{1,0:T(8,128)(2,1)}) %reduce-scatter.2.cloned.1.call-update) | async-done | bytes 262160 | tf_op jit(solution)/shard_map/reduce_scatter | solution.py:128
  358.8 1.8 convert_multiply_fusion
  (141 shorter events, 42.6 us)
Async XLA Ops:
  7.2 147.1 %copy-start = (bf16[1,1,512,2048]{3,2,1,0:T(8,128)(2,1)S(1)}, bf16[1,1,512,2048]{3,2,1,0:T(8,128)(2,1)}, u32[]{:S(2)}) copy-start(bf16[1,1,512,2048]{3,2,1,0:T(8,128)(2,1)} %param.10) | copy-start | bytes 6291460
  7.2 155.4 %all-gather.2.cloned.1.call-start = ((), (), s32[]{:S(2)}) async-start(), calls=%async_computation.8 | async-start | bytes 10485760 | tf_op jit(solution)/shard_map/all_gather | solution.py:79
  7.9 2.2 copy-start.27
  7.9 3.4 copy-start.28
  14.3 7.6 %copy-start.43 = (s32[4,4]{1,0:T(4,128)S(1)}, s32[4,4]{1,0:T(4,128)}, u32[]{:S(2)}) copy-start(s32[4,4]{1,0:T(4,128)} %param.12) | copy-start | bytes 196
  14.4 7.8 %copy-start.42 = (s32[8,8]{1,0:T(8,128)S(1)}, s32[8,8]{1,0:T(8,128)}, u32[]{:S(2)}) copy-start(s32[8,8]{1,0:T(8,128)} %param.13) | copy-start | bytes 772
  15.7 44.3 %all-to-all-start.1 = ((bf16[3,8,32,1024]{3,2,0,1:T(8,128)(2,1)}), bf16[3,8,32,1024]{3,2,0,1:T(8,128)(2,1)}, u32[]{:S(2)}, u32[]{:S(2)}) async-start(bf16[3,8,32,1024]{3,2,0,1:T(8,128)(2,1)} %copy.219), calls=%async_computation.1 | async-start | bytes 3145728 | tf_op jit(solution)/shard_map/all_to_all | solution.py:89
  22.2 186.8 %copy-start.39 = (pred[8,8]{0,1:T(8,128)(4,1)}, pred[8,8]{0,1:T(8,128)(4,1)S(1)}, u32[]{:S(2)}) copy-start(pred[8,8]{0,1:T(8,128)(4,1)S(1)} %copy.213) | copy-start | bytes 196
  25.3 39.2 %copy-start.5 = (bf16[1,1,512,1024]{2,3,1,0:T(8,128)(2,1)}, bf16[1,1,512,1024]{2,3,1,0:T(8,128)(2,1)S(1)}, u32[]{:S(2)}) copy-start(bf16[1,1,512,1024]{2,3,1,0:T(8,128)(2,1)S(1)} %copy.296) | copy-start | bytes 3145732
  59.9 42.4 %all-to-all-start = ((bf16[3,8,32,1024]{3,2,0,1:T(8,128)(2,1)}), bf16[3,8,32,1024]{3,2,0,1:T(8,128)(2,1)}, u32[]{:S(2)}, u32[]{:S(2)}) async-start(bf16[3,8,32,1024]{3,2,0,1:T(8,128)(2,1)} %copy.211), calls=%async_computation | async-start | bytes 3145728 | tf_op jit(solution)/shard_map/all_to_all | solution.py:89
  67.4 3.3 copy-start.1
  67.4 3.3 copy-start.18
  103.9 2.1 copy-start.14
  103.9 2.1 copy-start.16
  104.9 1.1 copy-start.25
  105.0 1.0 copy-start.24
  105.0 3.5 copy-start.31
  105.9 3.3 copy-start.3
  105.9 7.0 %copy-start.37 = (f32[32,8,8]{2,1,0:T(8,128)}, f32[32,8,8]{2,1,0:T(8,128)S(1)}, u32[]{:S(2)}) copy-start(f32[32,8,8]{2,1,0:T(8,128)S(1)} %get-tuple-element.40) | copy-start | bytes 24580
  108.0 1.2 copy-start.34
  108.5 0.8 copy-start.36
  109.2 0.8 copy-start.29
  115.0 0.8 copy-start.30
  121.2 30.8 %all-to-all-start.2 = ((bf16[8,2,32,1024]{3,2,1,0:T(8,128)(2,1)}), bf16[8,2,32,1024]{3,2,1,0:T(8,128)(2,1)}, u32[]{:S(2)}, u32[]{:S(2)}) async-start(bf16[8,2,32,1024]{3,2,1,0:T(8,128)(2,1)} %copy.225), calls=%async_computation.2 | async-start | bytes 2097152 | tf_op jit(solution)/shard_map/all_to_all | solution.py:113
  125.4 233.4 %reduce-scatter.2.cloned.1.call-start = ((), (), s32[]{:S(2)}) async-start(), calls=%async_computation.9 | async-start | bytes 8650752 | tf_op jit(solution)/shard_map/reduce_scatter | solution.py:128
  168.4 26.7 %all-to-all-start.3 = ((bf16[8,32,1024]{2,1,0:T(8,128)(2,1)}), bf16[8,32,1024]{2,1,0:T(8,128)(2,1)}, u32[]{:S(2)}, u32[]{:S(2)}) async-start(bf16[8,32,1024]{2,1,0:T(8,128)(2,1)} %get-tuple-element.37), calls=%async_computation.3 | async-start | bytes 1048576 | tf_op jit(solution)/shard_map/all_to_all | solution.py:133
  195.1 27.9 %all-to-all-start.5 = ((bf16[8,32,1024]{2,1,0:T(8,128)(2,1)}), bf16[8,32,1024]{2,1,0:T(8,128)(2,1)}, u32[]{:S(2)}, u32[]{:S(2)}) async-start(bf16[8,32,1024]{2,1,0:T(8,128)(2,1)} %get-tuple-element.36), calls=%async_computation.5 | async-start | bytes 1048576 | tf_op jit(solution)/shard_map/all_to_all | solution.py:133
  200.4 0.8 copy-start.9
  206.0 3.0 copy-start.4
  206.0 3.1 copy-start.10
  206.0 3.1 copy-start.33
  206.0 3.1 copy-start.35
  206.0 4.7 %copy-start.26 = (bf16[32,8,8,128]{3,2,1,0:T(8,128)(2,1)S(1)}, bf16[32,8,8,128]{3,2,1,0:T(8,128)(2,1)}, u32[]{:S(2)}) copy-start(bf16[32,8,8,128]{3,2,1,0:T(8,128)(2,1)} %copy-done.25) | copy-start | bytes 1572868
  209.9 0.8 copy-start.13
  223.0 59.4 %all-to-all-start.4 = ((bf16[3,8,32,1024]{3,2,0,1:T(8,128)(2,1)}), bf16[3,8,32,1024]{3,2,0,1:T(8,128)(2,1)}, u32[]{:S(2)}, u32[]{:S(2)}) async-start(bf16[3,8,32,1024]{3,2,0,1:T(8,128)(2,1)} %copy.242), calls=%async_computation.4 | async-start | bytes 3145728 | tf_op jit(solution)/shard_map/all_to_all | solution.py:141
  235.8 1.5 copy-start.21
  235.8 4.3 %copy-start.40 = (pred[8,8]{0,1:T(8,128)(4,1)S(1)}, pred[8,8]{0,1:T(8,128)(4,1)}, u32[]{:S(2)}) copy-start(pred[8,8]{0,1:T(8,128)(4,1)} %copy-done.39) | copy-start | bytes 196
  239.3 0.8 copy-start.7
  243.7 3.0 copy-start.8
  243.7 3.0 copy-start.32
  243.7 3.0 copy-start.41
  243.7 4.7 %copy-start.17 = (bf16[32,8,8,128]{3,2,1,0:T(8,128)(2,1)S(1)}, bf16[32,8,8,128]{3,2,1,0:T(8,128)(2,1)}, u32[]{:S(2)}) copy-start(bf16[32,8,8,128]{3,2,1,0:T(8,128)(2,1)} %copy.304) | copy-start | bytes 1572868
  247.6 0.8 copy-start.12
  248.4 3.5 copy-start.15
  255.1 33.1 %copy-start.19 = (bf16[1,1,512,1024]{2,3,1,0:T(8,128)(2,1)S(1)}, bf16[1,1,512,1024]{2,3,1,0:T(8,128)(2,1)}, u32[]{:S(2)}) copy-start(bf16[1,1,512,1024]{2,3,1,0:T(8,128)(2,1)} %copy.297) | copy-start | bytes 3145732
  255.1 33.1 %copy-start.38 = (f32[8,512,1]{1,0,2:T(8,128)S(1)}, f32[8,512,1]{1,0,2:T(8,128)}, u32[]{:S(2)}) copy-start(f32[8,512,1]{1,0,2:T(8,128)} %add_bitcast_fusion) | copy-start | bytes 49156
  282.4 62.1 %all-to-all-start.6 = ((bf16[3,8,32,1024]{3,2,0,1:T(8,128)(2,1)}), bf16[3,8,32,1024]{3,2,0,1:T(8,128)(2,1)}, u32[]{:S(2)}, u32[]{:S(2)}) async-start(bf16[3,8,32,1024]{3,2,0,1:T(8,128)(2,1)} %copy.254), calls=%async_computation.6 | async-start | bytes 3145728 | tf_op jit(solution)/shard_map/all_to_all | solution.py:141
  288.3 5.6 %copy-start.6 = (bf16[1,1,512,1024]{2,3,1,0:T(8,128)(2,1)S(1)}, bf16[1,1,512,1024]{2,3,1,0:T(8,128)(2,1)}, u32[]{:S(2)}) copy-start(bf16[1,1,512,1024]{2,3,1,0:T(8,128)(2,1)} %copy-done.5) | copy-start | bytes 3145732
  293.8 2.0 copy-start.2
  297.2 7.3 %copy-start.20 = (bf16[512,8,128]{0,2,1:T(8,128)(2,1)S(1)}, bf16[512,8,128]{0,2,1:T(8,128)(2,1)}, u32[]{:S(2)}) copy-start(bf16[512,8,128]{0,2,1:T(8,128)(2,1)} %copy.259) | copy-start | bytes 3145732
  344.5 1.9 copy-start.11
  346.7 1.5 copy-start.22
  348.2 1.5 copy-start.23
Sparse Core Ops, SparseCore 0:
  9.9 90.2 all-gather.1
  162.8 196.0 reduce-scatter.1
where the time goes:
time: 372 us; the launch traced here: 368 us
  waiting for transfers between devices  153 us (41%)
  local copies, waits for them, and re-layouts  75.6 us (20%)
  matrix products  65.5 us (18%)
  starting transfers between devices  34.4 us (9%)
  other arithmetic  24.4 us (7%)
  between operations  15 us (4%)
    all_to_all x2, waiting for transfers between devices, on_device(): lax.all_to_all(packed[j], 'seq', split_axis=1, concat_axis=1, tiled=True)  53 us
    all_to_all x2, waiting for transfers between devices, on_device(): lax.all_to_all(jnp.stack([g.reshape(rows, piece, half) for g in col_grads...  45.6 us
    all_to_all x1, waiting for transfers between devices, on_device(): lax.all_to_all(jnp.stack(col_back, axis=1), 'seq', split_axis=0, concat_a...  23.7 us
    all_to_all x2, waiting for transfers between devices, on_device(): lax.all_to_all(grad_col_part[j], 'seq', split_axis=0, concat_axis=0, tile...  22.1 us
    unnamed x102, local copies, waits for them, and re-layouts  20.3 us
    another operation x8, local copies, waits for them, and re-layouts, on_device(): jnp.stack([g.reshape(rows, piece, half) for g in col_grads])  13.2 us
    all_to_all x2, starting transfers between devices, on_device(): lax.all_to_all(packed[j], 'seq', split_axis=1, concat_axis=1, tiled=True)  10.9 us
    all_to_all x2, starting transfers between devices, on_device(): lax.all_to_all(jnp.stack([g.reshape(rows, piece, half) for g in col_grads...  10.3 us
  transfers between devices with their start and end apart: 9, of which 8 were waited for; matrix products, arithmetic and copies ran while one was open for 43% of the time, Pallas kernels for 0%

commit v1 on v0

--- a/solution.py
+++ b/solution.py
@@ -9,6 +9,29 @@
 BLK = 128
 masked_out = -1e30
 scale = 1.0 / math.sqrt(DH)
+
+
+def in_blocks(x, dim, count):
+    dims = x.shape
+    tiles = x.reshape(*dims[:dim], count, dims[dim] // count, *dims[dim + 1 :])
+    return jnp.moveaxis(tiles, dim, 0)
+
+
+def laid_out(blocks, dim):
+    blocks = jnp.moveaxis(blocks, 0, dim)
+    lengths = blocks.shape
+    return blocks.reshape(*lengths[:dim], lengths[dim] * lengths[dim + 1], *lengths[dim + 2 :])
+
+
+def swapped_with_each(value, axis, split_dim, concat_dim):
+    size, place = (lax.axis_size(axis), lax.axis_index(axis))
+    pieces = in_blocks(value, split_dim, size)
+    done = [pieces[place]]
+    for step in range(1, size):
+        sent = pieces[place ^ step]
+        done.append(lax.ppermute(sent, axis, [(i, i ^ step) for i in range(size)]))
+    pieces = jnp.stack(done)[place ^ jnp.arange(size)]
+    return laid_out(pieces, concat_dim)
 
 
 def row_permit(row_mask):
@@ -130,9 +153,9 @@
     ).astype(jnp.float32) * (1.0 / math.sqrt(tokens * devices_all))
     col_grads_back = []
     for j in range(chunks):
-        grad_cols = lax.all_to_all(
-            grad_col_part[j], "seq", split_axis=0, concat_axis=0, tiled=True
-        ).reshape(rows, piece, heads_half, DH)
+        grad_cols = swapped_with_each(grad_col_part[j], "seq", 0, 0).reshape(
+            rows, piece, heads_half, DH
+        )
         col_q, col_k, col_v, col_out, col_scores, col_total = col_state[j]
         col_grads = column_backward(
             col_q, col_k, col_v, col_out, grad_cols, col_scores, col_total, col_ok

time: 372 us -> 396 us (1.065)
  waiting for transfers between devices: 153 us -> 180 us
  starting transfers between devices: 34.4 us -> 38.9 us
  other arithmetic: 24.4 us -> 20.1 us
    ppermute x0 -> x14, waiting for transfers between devices: none -> 96.5 us  [swapped_with_each(): done.append(lax.ppermute(sent, axis, [(i, i ^ step) for i in range(size)]))]
    all_to_all x2, waiting for transfers between devices: 45.6 us -> 5.64 us  [on_device(): lax.all_to_all(jnp.stack([g.reshape(rows, piece, half) for g in col_grads...]
    all_to_all x2 -> x0, waiting for transfers between devices: 22.1 us -> none  [on_device(): lax.all_to_all(grad_col_part[j], 'seq', split_axis=0, concat_axis=0, tile...]
    ppermute x0 -> x14, starting transfers between devices: none -> 14.5 us  [swapped_with_each(): done.append(lax.ppermute(sent, axis, [(i, i ^ step) for i in range(size)]))]
    all_to_all x2 -> x0, starting transfers between devices: 8.31 us -> none  [on_device(): lax.all_to_all(grad_col_part[j], 'seq', split_axis=0, concat_axis=0, tile...]
    reduce_scatter x1, waiting for transfers between devices: 7.6 us -> 0.01 us  [on_device(): lax.psum_scatter(partial.astype(jnp.bfloat16), ('dp', 'seq'), scatter_dim...]
    unnamed x102 -> x126, local copies, waits for them, and re-layouts: 20.3 us -> 24.1 us
  transfers between devices with their start and end apart: 9 -> 21, of which waited for: 8 -> 12; matrix products, arithmetic and copies ran while one was open for 43% -> 37% of each run, Pallas kernels for 0% -> 0%
where the time goes in v1:
time: 396 us; the launch traced here: 391 us
  waiting for transfers between devices  180 us (45%)
  local copies, waits for them, and re-layouts  74.1 us (19%)
  matrix products  63.1 us (16%)
  starting transfers between devices  38.9 us (10%)
  other arithmetic  20.1 us (5%)
  between operations  15.1 us (4%)
    ppermute x14, waiting for transfers between devices, swapped_with_each(): done.append(lax.ppermute(sent, axis, [(i, i ^ step) for i in range(size)]))  96.5 us
    all_to_all x2, waiting for transfers between devices, on_device(): lax.all_to_all(packed[j], 'seq', split_axis=1, concat_axis=1, tiled=True)  53 us
    all_to_all x1, waiting for transfers between devices, on_device(): lax.all_to_all(jnp.stack(col_back, axis=1), 'seq', split_axis=0, concat_a...  24.1 us
    unnamed x126, local copies, waits for them, and re-layouts  24.1 us
    ppermute x14, starting transfers between devices, swapped_with_each(): done.append(lax.ppermute(sent, axis, [(i, i ^ step) for i in range(size)]))  14.5 us
    all_to_all x2, starting transfers between devices, on_device(): lax.all_to_all(packed[j], 'seq', split_axis=1, concat_axis=1, tiled=True)  11.1 us
    dot_general x1, matrix products, on_device(): jnp.dot(attention, weight, preferred_element_type=jnp.float32)  9.7 us
    another operation x8, local copies, waits for them, and re-layouts, on_device(): jnp.stack([g.reshape(rows, piece, half) for g in col_grads])  9.27 us
  transfers between devices with their start and end apart: 21, of which 12 were waited for; matrix products, arithmetic and copies ran while one was open for 37% of the time, Pallas kernels for 0%

profile of v1, /device:TPU:0, one launch (start us, length us, event | category | flops | bytes accessed | tf_op | source)
XLA Modules:
  0.0 391.3 jit_solution(4649671380392426734)
XLA Ops:
  7.9 1.9 fusion.100
  13.6 1.6 slice_bitcast_fusion.1
  16.5 6.3 %all-to-all-start.1 = ((bf16[3,8,32,1024]{3,2,0,1:T(8,128)(2,1)}), bf16[3,8,32,1024]{3,2,0,1:T(8,128)(2,1)}, u32[]{:S(2)}, u32[]{:S(2)}) async-start(bf16[3,8,32,1024]{3,2,0,1:T(8,128)(2,1)} %copy.216), calls=%async_computation.1 | async-start | bytes 3145728 | tf_op jit(solution)/shard_map/all_to_all | solution.py:112
  24.5 1.5 copy.292
  26.0 2.7 copy.293
  28.7 2.7 copy.208
  31.4 29.3 %all-to-all-done.1 = bf16[3,8,32,1024]{3,2,0,1:T(8,128)(2,1)} async-done(((bf16[3,8,32,1024]{3,2,0,1:T(8,128)(2,1)}), bf16[3,8,32,1024]{3,2,0,1:T(8,128)(2,1)}, u32[]{:S(2)}, u32[]{:S(2)}) %all-to-all-start.1) | async-done | bytes 1572896 | tf_op jit(solution)/shard_map/all_to_all | solution.py:112
  60.7 4.8 %all-to-all-start = ((bf16[3,8,32,1024]{3,2,0,1:T(8,128)(2,1)}), bf16[3,8,32,1024]{3,2,0,1:T(8,128)(2,1)}, u32[]{:S(2)}, u32[]{:S(2)}) async-start(bf16[3,8,32,1024]{3,2,0,1:T(8,128)(2,1)} %copy.208), calls=%async_computation | async-start | bytes 3145728 | tf_op jit(solution)/shard_map/all_to_all | solution.py:112
  65.5 2.9 select_reduce_fusion
  68.4 1.5 fusion
  71.7 3.6 fusion.36
  75.3 1.5 fusion.103
  79.6 23.7 %all-to-all-done = bf16[3,8,32,1024]{3,2,0,1:T(8,128)(2,1)} async-done(((bf16[3,8,32,1024]{3,2,0,1:T(8,128)(2,1)}), bf16[3,8,32,1024]{3,2,0,1:T(8,128)(2,1)}, u32[]{:S(2)}, u32[]{:S(2)}) %all-to-all-start) | async-done | bytes 1572896 | tf_op jit(solution)/shard_map/all_to_all | solution.py:112
  103.3 1.5 fusion.102
  107.0 2.0 fusion.54
  111.9 2.1 stack_reshape.25
  114.0 2.1 convolution_convert_fusion.4
  117.7 2.1 stack_reshape.24
  122.2 4.2 %all-to-all-start.2 = ((bf16[8,2,32,1024]{3,2,1,0:T(8,128)(2,1)}), bf16[8,2,32,1024]{3,2,1,0:T(8,128)(2,1)}, u32[]{:S(2)}, u32[]{:S(2)}) async-start(bf16[8,2,32,1024]{3,2,1,0:T(8,128)(2,1)} %copy.222), calls=%async_computation.2 | async-start | bytes 2097152 | tf_op jit(solution)/shard_map/all_to_all | solution.py:136
  126.6 2.3 copy.209
  128.9 24.1 %all-to-all-done.2 = bf16[8,2,32,1024]{3,2,1,0:T(8,128)(2,1)} async-done(((bf16[8,2,32,1024]{3,2,1,0:T(8,128)(2,1)}), bf16[8,2,32,1024]{3,2,1,0:T(8,128)(2,1)}, u32[]{:S(2)}, u32[]{:S(2)}) %all-to-all-start.2) | async-done | bytes 1048608 | tf_op jit(solution)/shard_map/all_to_all | solution.py:136
  153.0 2.3 copy.223
  155.3 8.3 %fusion.14 = bf16[2048,2048]{1,0:T(8,128)(2,1)} fusion(bf16[1,1,512,2048]{3,2,1,0:T(8,128)(2,1)S(1)} %copy-done, bf16[512,1024]{0,1:T(8,128)(2,1)} %copy.223, bf16[512,1024]{0,1:T(8,128)(2,1)} %bitcast.297), kind=kOutput, calls=%fused_computation.31 | convolution fusion | flops 4299161600 | bytes 12582912 | tf_op jit(solution)/shard_map/dot_general | solution.py:140
  164.3 1.8 log_add_fusion
  166.0 4.5 %fusion.31 = bf16[64,8,8,128]{3,1,2,0:T(8,128)(2,1)S(1)} fusion(bf16[2048,2048]{1,0:T(8,128)(2,1)} %all-gather.2.cloned.1.call-done, bf16[1,1,512,2048]{3,2,1,0:T(8,128)(2,1)S(1)} %copy-done), kind=kOutput, calls=%fused_computation.47 | convolution fusion | flops 2148007936 | bytes 7340032 | tf_op jit(solution)/shard_map/dot_general | solution.py:142
  171.8 2.4 copy.255
  174.3 4.6 %fusion.18 = bf16[1024,512]{0,1:T(8,128)(2,1)S(1)} fusion(bf16[1,1,512,2048]{3,2,1,0:T(8,128)(2,1)S(1)} %copy-done, bf16[2048,2048]{1,0:T(8,128)(2,1)} %all-gather.2.cloned.1.call-done), kind=kOutput, calls=%fused_computation.44 | convolution fusion | flops 2148007936 | bytes 7340032 | tf_op jit(solution)/shard_map/dot_general | solution.py:146
  183.0 2.1 collective-permute-start.12
  185.1 3.1 collective-permute-start.10
  188.3 9.2 %collective-permute-done.1 = bf16[1,32,1024]{2,1,0:T(8,128)(2,1)S(1)} collective-permute-done((bf16[1,32,1024]{2,1,0:T(8,128)(2,1)S(1)}, bf16[1,32,1024]{2,1,0:T(8,128)(2,1)S(1)}, u32[]{:S(2)}, u32[]{:S(2)}) %collective-permute-start.1) | collective-permute-done | bytes 65568 | tf_op jit(solution)/shard_map/ppermute | solution.py:32
  197.5 2.2 collective-permute-start.2
  199.8 4.9 %collective-permute-done.2 = bf16[1,32,1024]{2,1,0:T(8,128)(2,1)S(1)} collective-permute-done((bf16[1,32,1024]{2,1,0:T(8,128)(2,1)S(1)}, bf16[1,32,1024]{2,1,0:T(8,128)(2,1)S(1)}, u32[]{:S(2)}, u32[]{:S(2)}) %collective-permute-start.2) | collective-permute-done | bytes 65568 | tf_op jit(solution)/shard_map/ppermute | solution.py:32
  205.6 7.7 %collective-permute-done.3 = bf16[1,32,1024]{2,1,0:T(8,128)(2,1)S(1)} collective-permute-done((bf16[1,32,1024]{2,1,0:T(8,128)(2,1)S(1)}, bf16[1,32,1024]{2,1,0:T(8,128)(2,1)S(1)}, u32[]{:S(2)}, u32[]{:S(2)}) %collective-permute-start.3) | collective-permute-done | bytes 65568 | tf_op jit(solution)/shard_map/ppermute | solution.py:32
  213.4 8.2 %collective-permute-done.4 = bf16[1,32,1024]{2,1,0:T(8,128)(2,1)S(1)} collective-permute-done((bf16[1,32,1024]{2,1,0:T(8,128)(2,1)S(1)}, bf16[1,32,1024]{2,1,0:T(8,128)(2,1)S(1)}, u32[]{:S(2)}, u32[]{:S(2)}) %collective-permute-start.4) | collective-permute-done | bytes 65568 | tf_op jit(solution)/shard_map/ppermute | solution.py:32
  221.6 1.4 collective-permute-start.5
  222.9 6.0 %collective-permute-done.5 = bf16[1,32,1024]{2,1,0:T(8,128)(2,1)S(1)} collective-permute-done((bf16[1,32,1024]{2,1,0:T(8,128)(2,1)S(1)}, bf16[1,32,1024]{2,1,0:T(8,128)(2,1)S(1)}, u32[]{:S(2)}, u32[]{:S(2)}) %collective-permute-start.5) | collective-permute-done | bytes 65568 | tf_op jit(solution)/shard_map/ppermute | solution.py:32
  229.2 7.2 %collective-permute-done.6 = bf16[1,32,1024]{2,1,0:T(8,128)(2,1)S(1)} collective-permute-done((bf16[1,32,1024]{2,1,0:T(8,128)(2,1)S(1)}, bf16[1,32,1024]{2,1,0:T(8,128)(2,1)S(1)}, u32[]{:S(2)}, u32[]{:S(2)}) %collective-permute-start.6) | collective-permute-done | bytes 65568 | tf_op jit(solution)/shard_map/ppermute | solution.py:32
  237.2 1.7 gather_fusion
  239.0 1.6 fusion.49
  241.5 2.1 stack_reshape.28
  248.0 1.4 pad_maximum_fusion.2
  249.4 1.3 copy.238
  250.7 3.9 %all-to-all-start.3 = ((bf16[3,8,32,1024]{3,2,0,1:T(8,128)(2,1)}), bf16[3,8,32,1024]{3,2,0,1:T(8,128)(2,1)S(1)}, u32[]{:S(2)}, u32[]{:S(2)}) async-start(bf16[3,8,32,1024]{3,2,0,1:T(8,128)(2,1)} %copy.238), calls=%async_computation.3 | async-start | bytes 3145728 | tf_op jit(solution)/shard_map/all_to_all | solution.py:164
  254.6 2.0 collective-permute-start.8
  257.5 46.8 %collective-permute-done.8 = bf16[1,32,1024]{2,1,0:T(8,128)(2,1)S(1)} collective-permute-done((bf16[1,32,1024]{2,1,0:T(8,128)(2,1)}, bf16[1,32,1024]{2,1,0:T(8,128)(2,1)S(1)}, u32[]{:S(2)}, u32[]{:S(2)}) %collective-permute-start.8) | collective-permute-done | bytes 65568 | tf_op jit(solution)/shard_map/ppermute | solution.py:32
  304.3 1.5 collective-permute-start.9
  305.8 6.5 %collective-permute-done.9 = bf16[1,32,1024]{2,1,0:T(8,128)(2,1)S(1)} collective-permute-done((bf16[1,32,1024]{2,1,0:T(8,128)(2,1)}, bf16[1,32,1024]{2,1,0:T(8,128)(2,1)S(1)}, u32[]{:S(2)}, u32[]{:S(2)}) %collective-permute-start.9) | collective-permute-done | bytes 65568 | tf_op jit(solution)/shard_map/ppermute | solution.py:32
  315.7 1.5 gather_fusion.1
  320.4 2.1 stack_reshape.31
  322.6 1.8 multiply_reduce_fusion.1
  327.7 1.6 fusion.45
  332.2 4.9 %all-to-all-start.4 = ((bf16[3,8,32,1024]{3,2,0,1:T(8,128)(2,1)}), bf16[3,8,32,1024]{3,2,0,1:T(8,128)(2,1)}, u32[]{:S(2)}, u32[]{:S(2)}) async-start(bf16[3,8,32,1024]{3,2,0,1:T(8,128)(2,1)} %copy.250), calls=%async_computation.4 | async-start | bytes 3145728 | tf_op jit(solution)/shard_map/all_to_all | solution.py:164
  337.2 5.5 %multiply_convert_fusion = bf16[8,512,512]{1,2,0:T(8,128)(2,1)S(1)} fusion(f32[8,512,512]{1,2,0:T(8,128)} %copy-done.2, f32[8,512]{1,0:T(8,128)S(1)} %multiply_reduce_fusion, f32[8,512]{1,0:T(8,128)S(1)} %bitcast.304, pred[512,512]{0,1:T(8,128)(4,1)S(1)} %fusion.53, bf16[512,8,128]{0,2,1:T(8,128)(2,1)} %copy.255, bf16[512,8,128]{0,2,1:T(8,128)(2,1)S(1)} %bitcast.269), kind=kOutput, calls=%fused_computation.2 | convolution fusion | flops 547356672 | bytes 14974976 | tf_op jit(solution)/shard_map/ihd,jhd->hij/dot_general | solution.py:65
  344.7 1.3 copy.252
  346.1 3.8 multiply_convert_fusion.1
  351.2 6.1 %fusion.28 = bf16[8,128,512]{2,1,0:T(8,128)(2,1)} fusion(bf16[512,8,128]{0,2,1:T(8,128)(2,1)S(1)} %copy-done.18, f32[8,512,512]{1,2,0:T(8,128)} %copy-done.2, f32[8,512]{1,0:T(8,128)S(1)} %bitcast.305, pred[512,512]{0,1:T(8,128)(4,1)S(1)} %fusion.53), kind=kOutput, calls=%fused_computation.46 | convolution fusion | flops 543686656 | bytes 10764288 | tf_op jit(solution)/shard_map/hij,ihd->jhd/dot_general | solution.py:62
  357.3 2.3 copy.257
  359.5 9.7 %fusion.12 = bf16[1,1,512,2048]{3,2,1,0:T(8,128)(2,1)} fusion(bf16[2048,2048]{1,0:T(8,128)(2,1)} %all-gather.2.cloned.1.call-done, bf16[512,1024]{0,1:T(8,128)(2,1)} %copy.223, bf16[512,1024]{0,1:T(8,128)(2,1)S(1)} %bitcast.298), kind=kOutput, calls=%fused_computation.25 | convolution fusion | flops 4300210176 | bytes 12582912 | tf_op jit(solution)/shard_map/dot_general | solution.py:183
  369.4 5.6 %all-to-all-done.4 = bf16[3,8,32,1024]{3,2,0,1:T(8,128)(2,1)} async-done(((bf16[3,8,32,1024]{3,2,0,1:T(8,128)(2,1)}), bf16[3,8,32,1024]{3,2,0,1:T(8,128)(2,1)}, u32[]{:S(2)}, u32[]{:S(2)}) %all-to-all-start.4) | async-done | bytes 1572896 | tf_op jit(solution)/shard_map/all_to_all | solution.py:164
  375.1 1.6 copy.350
  377.9 1.5 maximum_bitcast_fusion.2
  379.4 1.5 maximum_bitcast_fusion
  380.9 1.5 maximum_bitcast_fusion.1
  382.4 1.8 convert_multiply_fusion
  (196 shorter events, 53.1 us)
Async XLA Ops:
  7.2 148.1 %copy-start = (bf16[1,1,512,2048]{3,2,1,0:T(8,128)(2,1)S(1)}, bf16[1,1,512,2048]{3,2,1,0:T(8,128)(2,1)}, u32[]{:S(2)}) copy-start(bf16[1,1,512,2048]{3,2,1,0:T(8,128)(2,1)} %param.10) | copy-start | bytes 6291460
  7.2 156.4 %all-gather.2.cloned.1.call-start = ((), (), s32[]{:S(2)}) async-start(), calls=%async_computation.6 | async-start | bytes 10485760 | tf_op jit(solution)/shard_map/all_gather | solution.py:102
  7.9 2.2 copy-start.28
  10.1 2.0 copy-start.29
  15.2 7.6 %copy-start.49 = (s32[4,4]{1,0:T(4,128)S(1)}, s32[4,4]{1,0:T(4,128)}, u32[]{:S(2)}) copy-start(s32[4,4]{1,0:T(4,128)} %param.12) | copy-start | bytes 196
  15.2 7.8 %copy-start.48 = (s32[8,8]{1,0:T(8,128)S(1)}, s32[8,8]{1,0:T(8,128)}, u32[]{:S(2)}) copy-start(s32[8,8]{1,0:T(8,128)} %param.13) | copy-start | bytes 772
  16.5 44.3 %all-to-all-start.1 = ((bf16[3,8,32,1024]{3,2,0,1:T(8,128)(2,1)}), bf16[3,8,32,1024]{3,2,0,1:T(8,128)(2,1)}, u32[]{:S(2)}, u32[]{:S(2)}) async-start(bf16[3,8,32,1024]{3,2,0,1:T(8,128)(2,1)} %copy.216), calls=%async_computation.1 | async-start | bytes 3145728 | tf_op jit(solution)/shard_map/all_to_all | solution.py:112
  23.0 90.9 %copy-start.45 = (pred[8,8]{0,1:T(8,128)(4,1)}, pred[8,8]{0,1:T(8,128)(4,1)S(1)}, u32[]{:S(2)}) copy-start(pred[8,8]{0,1:T(8,128)(4,1)S(1)} %copy.210) | copy-start | bytes 196
  26.0 39.5 %copy-start.7 = (bf16[1,1,512,1024]{2,3,1,0:T(8,128)(2,1)}, bf16[1,1,512,1024]{2,3,1,0:T(8,128)(2,1)S(1)}, u32[]{:S(2)}) copy-start(bf16[1,1,512,1024]{2,3,1,0:T(8,128)(2,1)S(1)} %copy.292) | copy-start | bytes 3145732
  60.7 42.6 %all-to-all-start = ((bf16[3,8,32,1024]{3,2,0,1:T(8,128)(2,1)}), bf16[3,8,32,1024]{3,2,0,1:T(8,128)(2,1)}, u32[]{:S(2)}, u32[]{:S(2)}) async-start(bf16[3,8,32,1024]{3,2,0,1:T(8,128)(2,1)} %copy.208), calls=%async_computation | async-start | bytes 3145728 | tf_op jit(solution)/shard_map/all_to_all | solution.py:112
  68.4 3.3 copy-start.2
  68.4 3.3 copy-start.16
  104.9 2.1 copy-start.12
  104.9 2.1 copy-start.14
  105.9 1.1 copy-start.26
  106.0 3.5 copy-start.33
  106.9 3.3 copy-start.5
  107.0 7.0 %copy-start.43 = (f32[32,8,8]{2,1,0:T(8,128)}, f32[32,8,8]{2,1,0:T(8,128)S(1)}, u32[]{:S(2)}) copy-start(f32[32,8,8]{2,1,0:T(8,128)S(1)} %get-tuple-element.56) | copy-start | bytes 24580
  109.0 1.2 copy-start.38
  122.2 30.8 %all-to-all-start.2 = ((bf16[8,2,32,1024]{3,2,1,0:T(8,128)(2,1)}), bf16[8,2,32,1024]{3,2,1,0:T(8,128)(2,1)}, u32[]{:S(2)}, u32[]{:S(2)}) async-start(bf16[8,2,32,1024]{3,2,1,0:T(8,128)(2,1)} %copy.222), calls=%async_computation.2 | async-start | bytes 2097152 | tf_op jit(solution)/shard_map/all_to_all | solution.py:136
  126.4 256.0 %reduce-scatter.2.cloned.1.call-start = ((), (), s32[]{:S(2)}) async-start(), calls=%async_computation.7 | async-start | bytes 8650752 | tf_op jit(solution)/shard_map/reduce_scatter | solution.py:151
  178.9 1.2 copy-start.4
  178.9 1.6 copy-start.19
  179.0 9.2 %collective-permute-start = (bf16[1,32,1024]{2,1,0:T(8,128)(2,1)S(1)}, bf16[1,32,1024]{2,1,0:T(8,128)(2,1)S(1)}, u32[]{:S(2)}, u32[]{:S(2)}) collective-permute-start(bf16[1,32,1024]{2,1,0:T(8,128)(2,1)S(1)} %get-tuple-element.52), channel_id=1, source_target_pairs={{0,1},{1,0},{2,3},{3,2},{4,5},{5,4},{6,7},{7,6},{8,9},{9,8},{10,11... | collective-permute-start | bytes 196616 | tf_op jit(solution)/shard_map/ppermute | solution.py:32
  180.4 58.6 %copy-start.6 = (f32[32,8,8,8]{2,3,1,0:T(8,128)S(1)}, f32[32,8,8,8]{2,3,1,0:T(8,128)}, u32[]{:S(2)}) copy-start(f32[32,8,8,8]{2,3,1,0:T(8,128)} %copy-done.5) | copy-start | bytes 196612
  182.1 132.7 %collective-permute-start.13 = (bf16[1,32,1024]{2,1,0:T(8,128)(2,1)}, bf16[1,32,1024]{2,1,0:T(8,128)(2,1)}, u32[]{:S(2)}, u32[]{:S(2)}) collective-permute-start(bf16[1,32,1024]{2,1,0:T(8,128)(2,1)} %get-tuple-element.38), channel_id=1, source_target_pairs={{0,7},{1,6},{2,5},{3,4},{4,3},{5,2},{6,1},{7,0},{8,15},{9,14},{10,... | collective-permute-start | bytes 196616 | tf_op jit(solution)/shard_map/ppermute | solution.py:32
  183.0 130.9 %collective-permute-start.12 = (bf16[1,32,1024]{2,1,0:T(8,128)(2,1)}, bf16[1,32,1024]{2,1,0:T(8,128)(2,1)}, u32[]{:S(2)}, u32[]{:S(2)}) collective-permute-start(bf16[1,32,1024]{2,1,0:T(8,128)(2,1)} %get-tuple-element.39), channel_id=1, source_target_pairs={{0,6},{1,7},{2,4},{3,5},{4,2},{5,3},{6,0},{7,1},{8,14},{9,15},{10,... | collective-permute-start | bytes 196616 | tf_op jit(solution)/shard_map/ppermute | solution.py:32
  185.1 128.0 %collective-permute-start.11 = (bf16[1,32,1024]{2,1,0:T(8,128)(2,1)}, bf16[1,32,1024]{2,1,0:T(8,128)(2,1)}, u32[]{:S(2)}, u32[]{:S(2)}) collective-permute-start(bf16[1,32,1024]{2,1,0:T(8,128)(2,1)} %get-tuple-element.40), channel_id=1, source_target_pairs={{0,5},{1,4},{2,7},{3,6},{4,1},{5,0},{6,3},{7,2},{8,13},{9,12},{10,... | collective-permute-start | bytes 196616 | tf_op jit(solution)/shard_map/ppermute | solution.py:32
  185.1 127.1 %collective-permute-start.10 = (bf16[1,32,1024]{2,1,0:T(8,128)(2,1)}, bf16[1,32,1024]{2,1,0:T(8,128)(2,1)}, u32[]{:S(2)}, u32[]{:S(2)}) collective-permute-start(bf16[1,32,1024]{2,1,0:T(8,128)(2,1)} %get-tuple-element.41), channel_id=1, source_target_pairs={{0,4},{1,5},{2,6},{3,7},{4,0},{5,1},{6,2},{7,3},{8,12},{9,13},{10,... | collective-permute-start | bytes 196616 | tf_op jit(solution)/shard_map/ppermute | solution.py:32
  188.3 9.3 %collective-permute-start.1 = (bf16[1,32,1024]{2,1,0:T(8,128)(2,1)S(1)}, bf16[1,32,1024]{2,1,0:T(8,128)(2,1)S(1)}, u32[]{:S(2)}, u32[]{:S(2)}) collective-permute-start(bf16[1,32,1024]{2,1,0:T(8,128)(2,1)S(1)} %get-tuple-element.51), channel_id=1, source_target_pairs={{0,2},{1,3},{2,0},{3,1},{4,6},{5,7},{6,4},{7,5},{8,10},{9,11},{10,... | collective-permute-start | bytes 196616 | tf_op jit(solution)/shard_map/ppermute | solution.py:32
  197.5 7.2 %collective-permute-start.2 = (bf16[1,32,1024]{2,1,0:T(8,128)(2,1)S(1)}, bf16[1,32,1024]{2,1,0:T(8,128)(2,1)S(1)}, u32[]{:S(2)}, u32[]{:S(2)}) collective-permute-start(bf16[1,32,1024]{2,1,0:T(8,128)(2,1)S(1)} %get-tuple-element.50), channel_id=1, source_target_pairs={{0,3},{1,2},{2,1},{3,0},{4,7},{5,6},{6,5},{7,4},{8,11},{9,10},{10,... | collective-permute-start | bytes 196616 | tf_op jit(solution)/shard_map/ppermute | solution.py:32
  204.7 8.6 %collective-permute-start.3 = (bf16[1,32,1024]{2,1,0:T(8,128)(2,1)S(1)}, bf16[1,32,1024]{2,1,0:T(8,128)(2,1)S(1)}, u32[]{:S(2)}, u32[]{:S(2)}) collective-permute-start(bf16[1,32,1024]{2,1,0:T(8,128)(2,1)S(1)} %get-tuple-element.49), channel_id=1, source_target_pairs={{0,4},{1,5},{2,6},{3,7},{4,0},{5,1},{6,2},{7,3},{8,12},{9,13},{10,... | collective-permute-start | bytes 196616 | tf_op jit(solution)/shard_map/ppermute | solution.py:32
  213.4 8.2 %collective-permute-start.4 = (bf16[1,32,1024]{2,1,0:T(8,128)(2,1)S(1)}, bf16[1,32,1024]{2,1,0:T(8,128)(2,1)S(1)}, u32[]{:S(2)}, u32[]{:S(2)}) collective-permute-start(bf16[1,32,1024]{2,1,0:T(8,128)(2,1)S(1)} %get-tuple-element.48), channel_id=1, source_target_pairs={{0,5},{1,4},{2,7},{3,6},{4,1},{5,0},{6,3},{7,2},{8,13},{9,12},{10,... | collective-permute-start | bytes 196616 | tf_op jit(solution)/shard_map/ppermute | solution.py:32
  221.6 7.4 %collective-permute-start.5 = (bf16[1,32,1024]{2,1,0:T(8,128)(2,1)S(1)}, bf16[1,32,1024]{2,1,0:T(8,128)(2,1)S(1)}, u32[]{:S(2)}, u32[]{:S(2)}) collective-permute-start(bf16[1,32,1024]{2,1,0:T(8,128)(2,1)S(1)} %get-tuple-element.47), channel_id=1, source_target_pairs={{0,6},{1,7},{2,4},{3,5},{4,2},{5,3},{6,0},{7,1},{8,14},{9,15},{10,... | collective-permute-start | bytes 196616 | tf_op jit(solution)/shard_map/ppermute | solution.py:32
  229.0 7.4 %collective-permute-start.6 = (bf16[1,32,1024]{2,1,0:T(8,128)(2,1)S(1)}, bf16[1,32,1024]{2,1,0:T(8,128)(2,1)S(1)}, u32[]{:S(2)}, u32[]{:S(2)}) collective-permute-start(bf16[1,32,1024]{2,1,0:T(8,128)(2,1)S(1)} %get-tuple-element.46), channel_id=1, source_target_pairs={{0,7},{1,6},{2,5},{3,4},{4,3},{5,2},{6,1},{7,0},{8,15},{9,14},{10,... | collective-permute-start | bytes 196616 | tf_op jit(solution)/shard_map/ppermute | solution.py:32
  236.3 18.3 %collective-permute-start.7 = (bf16[1,32,1024]{2,1,0:T(8,128)(2,1)}, bf16[1,32,1024]{2,1,0:T(8,128)(2,1)}, u32[]{:S(2)}, u32[]{:S(2)}) collective-permute-start(bf16[1,32,1024]{2,1,0:T(8,128)(2,1)} %get-tuple-element.44), channel_id=1, source_target_pairs={{0,1},{1,0},{2,3},{3,2},{4,5},{5,4},{6,7},{7,6},{8,9},{9,8},{10,11... | collective-permute-start | bytes 196616 | tf_op jit(solution)/shard_map/ppermute | solution.py:32
  239.0 4.6 %copy-start.32 = (bf16[32,8,128,8]{2,3,1,0:T(8,128)(2,1)S(1)}, bf16[32,8,128,8]{2,3,1,0:T(8,128)(2,1)}, u32[]{:S(2)}) copy-start(bf16[32,8,128,8]{2,3,1,0:T(8,128)(2,1)} %copy-done.31) | copy-start | bytes 1572868
  243.5 1.1 copy-start.37
  243.5 1.1 copy-start.46
  243.5 1.9 copy-start.27
  245.5 1.7 copy-start.25
  250.7 6.0 %copy-start.40 = (bf16[8,1,32,1024]{3,2,0,1:T(8,128)(2,1)S(1)}, bf16[8,1,32,1024]{3,2,0,1:T(8,128)(2,1)}, u32[]{:S(2)}) copy-start(bf16[8,1,32,1024]{3,2,0,1:T(8,128)(2,1)} %get-tuple-element.45) | copy-start | bytes 1572868
  250.7 81.5 %all-to-all-start.3 = ((bf16[3,8,32,1024]{3,2,0,1:T(8,128)(2,1)}), bf16[3,8,32,1024]{3,2,0,1:T(8,128)(2,1)S(1)}, u32[]{:S(2)}, u32[]{:S(2)}) async-start(bf16[3,8,32,1024]{3,2,0,1:T(8,128)(2,1)} %copy.238), calls=%async_computation.3 | async-start | bytes 3145728 | tf_op jit(solution)/shard_map/all_to_all | solution.py:164
  254.6 49.6 %collective-permute-start.8 = (bf16[1,32,1024]{2,1,0:T(8,128)(2,1)}, bf16[1,32,1024]{2,1,0:T(8,128)(2,1)S(1)}, u32[]{:S(2)}, u32[]{:S(2)}) collective-permute-start(bf16[1,32,1024]{2,1,0:T(8,128)(2,1)} %get-tuple-element.43), channel_id=1, source_target_pairs={{0,2},{1,3},{2,0},{3,1},{4,6},{5,7},{6,4},{7,5},{8,10},{9,11},{10,... | collective-permute-start | bytes 196616 | tf_op jit(solution)/shard_map/ppermute | solution.py:32
  304.3 8.0 %collective-permute-start.9 = (bf16[1,32,1024]{2,1,0:T(8,128)(2,1)}, bf16[1,32,1024]{2,1,0:T(8,128)(2,1)S(1)}, u32[]{:S(2)}, u32[]{:S(2)}) collective-permute-start(bf16[1,32,1024]{2,1,0:T(8,128)(2,1)} %get-tuple-element.42), channel_id=1, source_target_pairs={{0,3},{1,2},{2,1},{3,0},{4,7},{5,6},{6,5},{7,4},{8,11},{9,10},{10,... | collective-permute-start | bytes 196616 | tf_op jit(solution)/shard_map/ppermute | solution.py:32
  322.5 1.9 copy-start.34
  322.5 1.9 copy-start.47
  322.5 3.6 copy-start.15
  326.1 1.7 copy-start.13
  327.7 1.9 copy-start.36
  330.9 6.2 %copy-start.17 = (bf16[1,1,512,1024]{2,3,1,0:T(8,128)(2,1)S(1)}, bf16[1,1,512,1024]{2,3,1,0:T(8,128)(2,1)}, u32[]{:S(2)}) copy-start(bf16[1,1,512,1024]{2,3,1,0:T(8,128)(2,1)} %copy.293) | copy-start | bytes 3145732
  330.9 6.2 %copy-start.44 = (f32[8,512,1]{1,0,2:T(8,128)S(1)}, f32[8,512,1]{1,0,2:T(8,128)}, u32[]{:S(2)}) copy-start(f32[8,512,1]{1,0,2:T(8,128)} %add_bitcast_fusion) | copy-start | bytes 49156
  332.2 4.9 %copy-start.9 = (bf16[3,8,32,1024]{3,2,0,1:T(8,128)(2,1)}, bf16[3,8,32,1024]{3,2,0,1:T(8,128)(2,1)S(1)}, u32[]{:S(2)}) copy-start(bf16[3,8,32,1024]{3,2,0,1:T(8,128)(2,1)S(1)} %all-to-all-done.3) | copy-start | bytes 4718596
  332.2 42.8 %all-to-all-start.4 = ((bf16[3,8,32,1024]{3,2,0,1:T(8,128)(2,1)}), bf16[3,8,32,1024]{3,2,0,1:T(8,128)(2,1)}, u32[]{:S(2)}, u32[]{:S(2)}) async-start(bf16[3,8,32,1024]{3,2,0,1:T(8,128)(2,1)} %copy.250), calls=%async_computation.4 | async-start | bytes 3145728 | tf_op jit(solution)/shard_map/all_to_all | solution.py:164
  337.2 5.5 %copy-start.8 = (bf16[1,1,512,1024]{2,3,1,0:T(8,128)(2,1)S(1)}, bf16[1,1,512,1024]{2,3,1,0:T(8,128)(2,1)}, u32[]{:S(2)}) copy-start(bf16[1,1,512,1024]{2,3,1,0:T(8,128)(2,1)} %copy-done.7) | copy-start | bytes 3145732
  342.7 2.1 copy-start.3
  342.7 3.4 copy-start.23
  346.1 5.1 %copy-start.18 = (bf16[512,8,128]{0,2,1:T(8,128)(2,1)S(1)}, bf16[512,8,128]{0,2,1:T(8,128)(2,1)}, u32[]{:S(2)}) copy-start(bf16[512,8,128]{0,2,1:T(8,128)(2,1)} %copy.255) | copy-start | bytes 3145732
  351.2 8.4 %copy-start.39 = (bf16[512,8,128]{0,2,1:T(8,128)(2,1)S(1)}, bf16[512,8,128]{0,2,1:T(8,128)(2,1)}, u32[]{:S(2)}) copy-start(bf16[512,8,128]{0,2,1:T(8,128)(2,1)} %copy.209) | copy-start | bytes 3145732
  359.5 9.7 %copy-start.10 = (bf16[3,8,32,1024]{3,2,0,1:T(8,128)(2,1)S(1)}, bf16[3,8,32,1024]{3,2,0,1:T(8,128)(2,1)}, u32[]{:S(2)}) copy-start(bf16[3,8,32,1024]{3,2,0,1:T(8,128)(2,1)} %copy-done.9) | copy-start | bytes 4718596
  376.7 1.2 copy-start.22
  377.0 2.4 copy-start.20
  379.4 1.5 copy-start.21
  379.4 4.8 %copy-start.1 = (bf16[1,1,512,2048]{3,2,1,0:T(8,128)(2,1)S(1)}, bf16[1,1,512,2048]{3,2,1,0:T(8,128)(2,1)}, u32[]{:S(2)}) copy-start(bf16[1,1,512,2048]{3,2,1,0:T(8,128)(2,1)} %param.10) | copy-start | bytes 6291460
  (7 other events, 6.0 us)
Sparse Core Ops, SparseCore 0:
  9.9 90.2 all-gather.1
  163.7 168.3 reduce-scatter.1
